TPU v7x, 256 devices: a whole 4x4x8 slice. The times are simulated.
256 devices in a mesh: expert: 32 (over z_hi, y, core), dp: 8 (over z_lo, x).
Axes of the slice: x: 4, y: 4, z: 8 (z_hi: 4, z_lo: 2; z = z_hi * 2 + z_lo), core: 2. Of those that a mesh axis runs over, the one named last changes fastest.
Arguments:
- tokens: bfloat16 [2048, 196, 384], P(('expert', 'dp')), may hold values from -6 to 6
- router: bfloat16 [384, 64], replicated, may hold values from -1 to 65
- expert_in: bfloat16 [64, 384, 1536], P('expert'), may hold values from -2.5 to 2.5
- expert_out: bfloat16 [64, 1536, 384], P('expert'), may hold values from -0.15625 to 0.15625
- out_grad: bfloat16 [2048, 196, 384], P(('expert', 'dp')), may hold values from -6 to 6
Outputs:
- grad_tokens: bfloat16 [2048, 196, 384], P(('expert', 'dp'))
- grad_in: float32 [64, 384, 1536], P('expert', None, 'dp')
- grad_out: float32 [64, 1536, 384], P('expert', 'dp')
- grad_router: float32 [384, 64], replicated
All inputs are finite; a program needn't handle non-finite values.
Results may differ from a plain program's by a relative error of at most 0.017.
Values may be sent and summed in bfloat16 or wider, within the bound.
No kernel may reach another device: no remote copies, remote signals or barrier semaphores. Data moves between devices by JAX's collectives and lax.ppermute only.
A program may use at most 64 MiB of HBM per device.

v0:
```python
import jax
import jax.numpy as jnp
from jax import lax
from jax.sharding import PartitionSpec as P


def on_device(tokens, router, expert_in, expert_out, out_grad):
    logits = jnp.einsum("bpd,ds->bps", tokens, router, preferred_element_type=jnp.float32)
    dispatch = jax.nn.softmax(logits, axis=1)
    combine = jax.nn.softmax(logits, axis=2)
    dispatch_low = dispatch.astype(jnp.bfloat16)
    combine_low = combine.astype(jnp.bfloat16)
    slots = jnp.einsum(
        "bps,bpd->bsd", dispatch_low, tokens, preferred_element_type=jnp.float32
    ).astype(jnp.bfloat16)
    slot_grads = jnp.einsum(
        "bps,bpd->bsd", combine_low, out_grad, preferred_element_type=jnp.float32
    ).astype(jnp.bfloat16)
    slots_here, grads_here = (
        lax.all_to_all(slots, "expert", split_axis=1, concat_axis=0, tiled=True),
        lax.all_to_all(slot_grads, "expert", split_axis=1, concat_axis=0, tiled=True),
    )
    hidden = jnp.einsum("rjd,jdf->rjf", slots_here, expert_in, preferred_element_type=jnp.float32)
    activated, gelu_back = jax.vjp(jax.nn.gelu, hidden)
    activated_low = activated.astype(jnp.bfloat16)
    outputs_here = jnp.einsum(
        "rjf,jfd->rjd", activated_low, expert_out, preferred_element_type=jnp.float32
    ).astype(jnp.bfloat16)
    act_grad = jnp.einsum(
        "rjd,jfd->rjf", grads_here, expert_out, preferred_element_type=jnp.float32
    )
    hidden_grad = gelu_back(act_grad)[0].astype(jnp.bfloat16)
    input_grad_here = jnp.einsum(
        "rjf,jdf->rjd", hidden_grad, expert_in, preferred_element_type=jnp.float32
    ).astype(jnp.bfloat16)
    outputs, inputs_grad = (
        lax.all_to_all(outputs_here, "expert", split_axis=0, concat_axis=1, tiled=True),
        lax.all_to_all(input_grad_here, "expert", split_axis=0, concat_axis=1, tiled=True),
    )
    first_term = jnp.einsum(
        "rjd,rjf->jdf", slots_here, hidden_grad, preferred_element_type=jnp.float32
    )
    second_term = jnp.einsum(
        "rjf,rjd->jfd", activated_low, grads_here, preferred_element_type=jnp.float32
    )
    grad_in = lax.psum_scatter(
        first_term.astype(jnp.bfloat16), "dp", scatter_dimension=2, tiled=True
    ).astype(jnp.float32)
    grad_out = lax.psum_scatter(
        second_term.astype(jnp.bfloat16), "dp", scatter_dimension=1, tiled=True
    ).astype(jnp.float32)
    combine_grad = jnp.einsum("bpd,bsd->bps", out_grad, outputs, preferred_element_type=jnp.float32)
    dispatch_grad = jnp.einsum(
        "bpd,bsd->bps", tokens, inputs_grad, preferred_element_type=jnp.float32
    )
    logit_grad = dispatch * (
        dispatch_grad - jnp.sum(dispatch * dispatch_grad, axis=1, keepdims=True)
    )
    logit_grad = logit_grad + combine * (
        combine_grad - jnp.sum(combine * combine_grad, axis=2, keepdims=True)
    )
    logit_low = logit_grad.astype(jnp.bfloat16)
    first_part = jnp.einsum(
        "bps,bsd->bpd", dispatch_low, inputs_grad, preferred_element_type=jnp.float32
    )
    second_part = jnp.einsum("bps,ds->bpd", logit_low, router, preferred_element_type=jnp.float32)
    grad_tokens = (first_part + second_part).astype(jnp.bfloat16)
    router_term = jnp.einsum("bpd,bps->ds", tokens, logit_low, preferred_element_type=jnp.float32)
    grad_router = lax.psum(router_term, ("expert", "dp"))
    return (grad_tokens, grad_in, grad_out, grad_router)


def solution(mesh):
    placed = (
        P(("expert", "dp"), None, None),
        P(),
        P("expert", None, None),
        P("expert", None, None),
        P(("expert", "dp"), None, None),
    )
    return jax.shard_map(
        on_device,
        mesh=mesh,
        in_specs=placed,
        out_specs=(
            P(("expert", "dp"), None, None),
            P("expert", None, "dp"),
            P("expert", "dp", None),
            P(),
        ),
        check_vma=False,
    )
```

profile of v0, /device:TPU:1, one launch (start us, length us, event | category | flops | bytes accessed | tf_op | source)
XLA Modules:
  0.0 387.2 jit_solution(1332848046215882536)
XLA Ops:
  8.0 2.8 fusion.56
  10.8 0.1 copy.44
  10.9 1.5 copy.40
  12.3 0.3 fusion.30
  12.6 1.8 convolution_convert_fusion.4
  14.5 1.0 copy.27
  15.5 12.8 %all-to-all-start.1 = ((bf16[8,64,384]{2,0,1:T(8,128)(2,1)}), bf16[8,64,384]{2,0,1:T(8,128)(2,1)S(1)}, u32[]{:S(2)}, u32[]{:S(2)}) async-start(bf16[8,64,384]{2,0,1:T(8,128)(2,1)} %copy.27), calls=%async_computation.1 | async-start | bytes 786432 | tf_op jit(solution)/shard_map/all_to_all | solution.py:20
  28.2 1.8 convolution_convert_fusion.5
  30.0 1.0 copy.24
  31.0 13.3 %all-to-all-done.1 = bf16[8,64,384]{2,0,1:T(8,128)(2,1)S(1)} async-done(((bf16[8,64,384]{2,0,1:T(8,128)(2,1)}), bf16[8,64,384]{2,0,1:T(8,128)(2,1)S(1)}, u32[]{:S(2)}, u32[]{:S(2)}) %all-to-all-start.1) | async-done | bytes 393248 | tf_op jit(solution)/shard_map/all_to_all | solution.py:20
  44.3 4.4 %all-to-all-start = ((bf16[8,64,384]{2,0,1:T(8,128)(2,1)}), bf16[8,64,384]{2,0,1:T(8,128)(2,1)}, u32[]{:S(2)}, u32[]{:S(2)}) async-start(bf16[8,64,384]{2,0,1:T(8,128)(2,1)} %copy.24), calls=%async_computation | async-start | bytes 786432 | tf_op jit(solution)/shard_map/all_to_all | solution.py:21
  48.6 0.0 reduce-scatter.5.cloned.1.call-start
  48.7 4.3 %convolution_bitcast_fusion = f32[256,2,1536]{2,0,1:T(8,128)} fusion(bf16[2,384,1536]{2,1,0:T(8,128)(2,1)} %param.7, bf16[8,32,2,384]{3,0,2,1:T(8,128)(2,1)S(1)} %bitcast.59), kind=kOutput, calls=%fused_computation.6 | convolution fusion | flops 603979776 | bytes 5898240 | tf_op jit(solution)/shard_map/rjd,jdf->rjf/dot_general | solution.py:23
  53.0 10.9 %all-to-all-done = bf16[8,64,384]{2,0,1:T(8,128)(2,1)} async-done(((bf16[8,64,384]{2,0,1:T(8,128)(2,1)}), bf16[8,64,384]{2,0,1:T(8,128)(2,1)}, u32[]{:S(2)}, u32[]{:S(2)}) %all-to-all-start) | async-done | bytes 393248 | tf_op jit(solution)/shard_map/all_to_all | solution.py:21
  63.8 4.8 %convolution_convert_fusion = bf16[2,1536,384]{2,1,0:T(8,128)(2,1)} fusion(bf16[8,32,2,384]{3,0,2,1:T(8,128)(2,1)} %bitcast.1, f32[256,2,1536]{2,0,1:T(8,128)} %convolution_bitcast_fusion), kind=kOutput, calls=%fused_computation.4 | convolution fusion | flops 612237312 | bytes 5898240 | tf_op jit(solution)/shard_map/rjf,rjd->jfd/dot_general | solution.py:43
  68.6 0.0 reduce-scatter.5.cloned.1.call-update
  68.7 0.0 reduce-scatter.3.cloned.1.call-start
  68.7 4.2 %fusion.8 = bf16[256,2,1536]{2,0,1:T(8,128)(2,1)S(1)} fusion(f32[256,2,1536]{2,0,1:T(8,128)} %convolution_bitcast_fusion, bf16[2,1536,384]{2,1,0:T(8,128)(2,1)S(1)} %copy-done, bf16[8,32,2,384]{3,0,2,1:T(8,128)(2,1)} %bitcast.1), kind=kOutput, calls=%fused_computation.14 | convolution fusion | flops 619708416 | bytes 7471104 | tf_op jit(solution)/shard_map/rjd,jfd->rjf/dot_general | solution.py:29
  72.9 1.2 copy-done.2
  74.1 2.4 convolution_convert_fusion.1
  76.6 0.0 reduce-scatter.3.cloned.1.call-update
  76.6 3.1 fusion.16
  79.8 1.2 copy.32
  80.9 4.7 %all-to-all-start.3 = ((bf16[256,2,384]{2,1,0:T(2,128)(2,1)}), bf16[256,2,384]{2,1,0:T(2,128)(2,1)S(1)}, u32[]{:S(2)}, u32[]{:S(2)}) async-start(bf16[256,2,384]{2,1,0:T(2,128)(2,1)} %copy.32), calls=%async_computation.3 | async-start | bytes 786432 | tf_op jit(solution)/shard_map/all_to_all | solution.py:37
  85.6 3.2 fusion.15
  88.8 1.2 copy.29
  90.0 14.7 %all-to-all-done.3 = bf16[256,2,384]{2,1,0:T(2,128)(2,1)S(1)} async-done(((bf16[256,2,384]{2,1,0:T(2,128)(2,1)}), bf16[256,2,384]{2,1,0:T(2,128)(2,1)S(1)}, u32[]{:S(2)}, u32[]{:S(2)}) %all-to-all-start.3) | async-done | bytes 393248 | tf_op jit(solution)/shard_map/all_to_all | solution.py:37
  104.7 5.1 %all-to-all-start.2 = ((bf16[256,2,384]{2,1,0:T(2,128)(2,1)}), bf16[256,2,384]{2,1,0:T(2,128)(2,1)}, u32[]{:S(2)}, u32[]{:S(2)}) async-start(bf16[256,2,384]{2,1,0:T(2,128)(2,1)} %copy.29), calls=%async_computation.2 | async-start | bytes 786432 | tf_op jit(solution)/shard_map/all_to_all | solution.py:38
  109.8 0.2 all-reduce.2.cloned.1.call-start
  110.0 1.1 copy.73
  111.0 1.9 all_to_all.67
  112.9 13.2 %all-to-all-done.2 = bf16[256,2,384]{2,1,0:T(2,128)(2,1)} async-done(((bf16[256,2,384]{2,1,0:T(2,128)(2,1)}), bf16[256,2,384]{2,1,0:T(2,128)(2,1)}, u32[]{:S(2)}, u32[]{:S(2)}) %all-to-all-start.2) | async-done | bytes 393248 | tf_op jit(solution)/shard_map/all_to_all | solution.py:38
  126.1 2.0 copy.74
  128.1 1.1 all_to_all.63
  129.3 2.0 convolution_bitcast_fusion.2
  131.3 1.0 fusion.13
  132.3 0.5 copy-done.1
  132.8 1.4 convolution_bitcast_fusion.3
  134.2 5.2 %convolution_bitcast_fusion.4 = f32[384,64]{0,1:T(8,128)} fusion(f32[8,196,64]{1,2,0:T(8,128)} %fusion.13, f32[8,196,64]{1,2,0:T(8,128)} %convolution_bitcast_fusion.3, bf16[8,196,384]{2,0,1:T(8,128)(2,1)} %param.5, f32[8,196,64]{1,2,0:T(8,128)S(1)} %copy.40, f32[8,64]{1,0:T(8,128)S(1)} %get-tuple-element.15, f32[8,64]{1,0:T(8,128)S(1)} %get-tuple-element.13), kind=kOutput, calls=%fused_computation.31 | convolution fusion | flops 77974208 | bytes 2510848 | tf_op jit(solution)/shard_map/bpd,bps->ds/dot_general | solution.py:68
  139.5 2.5 fusion.40
  142.0 0.0 all-reduce.2.cloned.1.call-update
  142.0 6.1 %add_convert_fusion = bf16[8,196,384]{2,1,0:T(8,128)(2,1)} fusion(f32[8,196,384]{2,1,0:T(8,128)} %fusion.40, f32[8,196,64]{1,2,0:T(8,128)} %fusion.13, f32[8,196,64]{1,2,0:T(8,128)} %convolution_bitcast_fusion.3, bf16[384,64]{0,1:T(8,128)(2,1)S(1)} %copy-done.3, f32[8,196,64]{1,2,0:T(8,128)S(1)} %copy.40, f32[8,64]{1,0:T(8,128)S(1)} %get-tuple-element.15, ...), kind=kOutput, calls=%fused_computation.16 | convolution fusion | flops 79178432 | bytes 4870144 | tf_op jit(solution)/shard_map/bps,ds->bpd/dot_general | solution.py:66
  148.1 2.5 copy.38
  150.5 1.8 convert_element_type.63
  152.4 13.2 %reduce-scatter.3.cloned.1.call-done = bf16[2,384,192]{1,2,0:T(8,128)(2,1)} async-done(((bf16[2,384,1536]{1,2,0:T(8,128)(2,1)}), bf16[2,384,192]{1,2,0:T(8,128)(2,1)}) %reduce-scatter.3.cloned.1.call-update) | async-done | bytes 294928 | tf_op jit(solution)/shard_map/reduce_scatter | solution.py:46
  165.6 1.8 convert_element_type.61
  167.4 210.8 %all-reduce.2.cloned.1.call-done = f32[384,64]{0,1:T(8,128)} async-done(((f32[384,64]{0,1:T(8,128)}), f32[384,64]{0,1:T(8,128)}) %all-reduce.2.cloned.1.call-update) | async-done | bytes 98320 | tf_op jit(solution)/shard_map/psum | solution.py:69
  378.2 1.5 copy.76
  (7 shorter events, 0.0 us)
Async XLA Ops:
  8.0 60.7 %copy-start = (bf16[2,1536,384]{2,1,0:T(8,128)(2,1)S(1)}, bf16[2,1536,384]{2,1,0:T(8,128)(2,1)}, u32[]{:S(2)}) copy-start(bf16[2,1536,384]{2,1,0:T(8,128)(2,1)} %param.8) | copy-start | bytes 7077892
  15.5 28.8 %all-to-all-start.1 = ((bf16[8,64,384]{2,0,1:T(8,128)(2,1)}), bf16[8,64,384]{2,0,1:T(8,128)(2,1)S(1)}, u32[]{:S(2)}, u32[]{:S(2)}) async-start(bf16[8,64,384]{2,0,1:T(8,128)(2,1)} %copy.27), calls=%async_computation.1 | async-start | bytes 786432 | tf_op jit(solution)/shard_map/all_to_all | solution.py:20
  44.3 19.6 %all-to-all-start = ((bf16[8,64,384]{2,0,1:T(8,128)(2,1)}), bf16[8,64,384]{2,0,1:T(8,128)(2,1)}, u32[]{:S(2)}, u32[]{:S(2)}) async-start(bf16[8,64,384]{2,0,1:T(8,128)(2,1)} %copy.24), calls=%async_computation | async-start | bytes 786432 | tf_op jit(solution)/shard_map/all_to_all | solution.py:21
  48.6 101.9 %reduce-scatter.5.cloned.1.call-start = ((), (), s32[]{:S(2)}) async-start(), calls=%async_computation.7 | async-start | bytes 2654208 | tf_op jit(solution)/shard_map/reduce_scatter | solution.py:49
  68.7 96.9 %reduce-scatter.3.cloned.1.call-start = ((), (), s32[]{:S(2)}) async-start(), calls=%async_computation.6 | async-start | bytes 2654208 | tf_op jit(solution)/shard_map/reduce_scatter | solution.py:46
  72.9 1.2 copy-start.2
  80.9 23.8 %all-to-all-start.3 = ((bf16[256,2,384]{2,1,0:T(2,128)(2,1)}), bf16[256,2,384]{2,1,0:T(2,128)(2,1)S(1)}, u32[]{:S(2)}, u32[]{:S(2)}) async-start(bf16[256,2,384]{2,1,0:T(2,128)(2,1)} %copy.32), calls=%async_computation.3 | async-start | bytes 786432 | tf_op jit(solution)/shard_map/all_to_all | solution.py:37
  104.7 21.4 %all-to-all-start.2 = ((bf16[256,2,384]{2,1,0:T(2,128)(2,1)}), bf16[256,2,384]{2,1,0:T(2,128)(2,1)}, u32[]{:S(2)}, u32[]{:S(2)}) async-start(bf16[256,2,384]{2,1,0:T(2,128)(2,1)} %copy.29), calls=%async_computation.2 | async-start | bytes 786432 | tf_op jit(solution)/shard_map/all_to_all | solution.py:38
  109.8 268.4 %all-reduce.2.cloned.1.call-start = ((), (), s32[]{:S(2)}) async-start(), calls=%async_computation.8 | async-start | bytes 196608 | tf_op jit(solution)/shard_map/psum | solution.py:69
  131.3 1.5 copy-start.1
  139.5 2.5 copy-start.3
Sparse Core Ops, SparseCore 0:
  68.8 45.1 reduce-scatter.4
  116.6 48.9 reduce-scatter.2
Sparse Core Ops, SparseCore 1:
  142.1 236.1 all-reduce.1
where the time goes:
time: 388 us; the launch traced here: 387 us
  waiting for transfers between devices  276 us (71%)
  matrix products  45.7 us (12%)
  starting transfers between devices  27.2 us (7%)
  local copies, waits for them, and re-layouts  17.6 us (5%)
  between operations  15.6 us (4%)
  other arithmetic  4.88 us (1%)
    psum x1, waiting for transfers between devices, on_device(): grad_router = lax.psum(router_term, ('expert', 'dp'))  211 us
    all_to_all x1, waiting for transfers between devices, on_device(): lax.all_to_all(outputs_here, 'expert', split_axis=0, concat_axis=1, tiled...  14.7 us
    all_to_all x1, waiting for transfers between devices, on_device(): lax.all_to_all(slots, 'expert', split_axis=1, concat_axis=0, tiled=True)  13.3 us
    reduce_scatter x1, waiting for transfers between devices, on_device(): lax.psum_scatter(first_term.astype(jnp.bfloat16), 'dp', scatter_dimension...  13.2 us
    all_to_all x1, waiting for transfers between devices, on_device(): lax.all_to_all(input_grad_here, 'expert', split_axis=0, concat_axis=1, ti...  13.2 us
    all_to_all x1, starting transfers between devices, on_device(): lax.all_to_all(slots, 'expert', split_axis=1, concat_axis=0, tiled=True)  12.8 us
    all_to_all x1, waiting for transfers between devices, on_device(): lax.all_to_all(slot_grads, 'expert', split_axis=1, concat_axis=0, tiled=T...  10.9 us
  transfers between devices with their start and end apart: 7, of which 6 were waited for; matrix products, arithmetic and copies ran while one was open for 13% of the time, Pallas kernels for 0%

commit v1 on v0

--- a/solution.py
+++ b/solution.py
@@ -66,7 +66,7 @@
     second_part = jnp.einsum("bps,ds->bpd", logit_low, router, preferred_element_type=jnp.float32)
     grad_tokens = (first_part + second_part).astype(jnp.bfloat16)
     router_term = jnp.einsum("bpd,bps->ds", tokens, logit_low, preferred_element_type=jnp.float32)
-    grad_router = lax.psum(router_term, ("expert", "dp"))
+    grad_router = jnp.sum(lax.all_gather(router_term, ("expert", "dp")), axis=0)
     return (grad_tokens, grad_in, grad_out, grad_router)
 
 

time: 388 us -> 904 us (2.33)
  waiting for transfers between devices: 276 us -> 788 us
    all_gather x0 -> x1, waiting for transfers between devices: none -> 704 us  [on_device(): grad_router = jnp.sum(lax.all_gather(router_term, ('expert', 'dp')), axis=0)]
    psum x1 -> x0, waiting for transfers between devices: 211 us -> none  [on_device(): grad_router = lax.psum(router_term, ('expert', 'dp'))]
    reduce_scatter x1, waiting for transfers between devices: 0.01 us -> 24.1 us  [on_device(): lax.psum_scatter(second_term.astype(jnp.bfloat16), 'dp', scatter_dimensio...]
    reduce_scatter x1, waiting for transfers between devices: 13.2 us -> 0.01 us  [on_device(): lax.psum_scatter(first_term.astype(jnp.bfloat16), 'dp', scatter_dimension...]
    unnamed x11 -> x13, local copies, waits for them, and re-layouts: 5.8 us -> 15.8 us
  transfers between devices with their start and end apart: 7 -> 7, of which waited for: 6 -> 6; matrix products, arithmetic and copies ran while one was open for 13% -> 4% of each run, Pallas kernels for 0% -> 0%
where the time goes in v1:
time: 904 us; the launch traced here: 900 us
  waiting for transfers between devices  788 us (87%)
  matrix products  41.1 us (5%)
  starting transfers between devices  25.1 us (3%)
  local copies, waits for them, and re-layouts  22.3 us (2%)
  between operations  15.7 us (2%)
    all_gather x1, waiting for transfers between devices, on_device(): grad_router = jnp.sum(lax.all_gather(router_term, ('expert', 'dp')), axis=0)  704 us
    reduce_scatter x1, waiting for transfers between devices, on_device(): lax.psum_scatter(second_term.astype(jnp.bfloat16), 'dp', scatter_dimensio...  24.1 us
    all_to_all x1, waiting for transfers between devices, on_device(): lax.all_to_all(outputs_here, 'expert', split_axis=0, concat_axis=1, tiled...  19.4 us
  transfers between devices with their start and end apart: 7, of which 6 were waited for; matrix products, arithmetic and copies ran while one was open for 4% of the time, Pallas kernels for 0%

profile of v1, /device:TPU:1, one launch (start us, length us, event | category | flops | bytes accessed | tf_op | source)
XLA Modules:
  0.0 900.4 jit_solution(6414002050279115386)
XLA Ops:
  8.0 2.8 fusion.56
  10.8 1.5 copy.40
  12.3 0.1 copy.44
  12.3 0.3 fusion.30
  12.6 1.8 convolution_convert_fusion.4
  14.5 1.0 copy.27
  15.5 12.8 %all-to-all-start.1 = ((bf16[8,64,384]{2,0,1:T(8,128)(2,1)}), bf16[8,64,384]{2,0,1:T(8,128)(2,1)S(1)}, u32[]{:S(2)}, u32[]{:S(2)}) async-start(bf16[8,64,384]{2,0,1:T(8,128)(2,1)} %copy.27), calls=%async_computation.1 | async-start | bytes 786432 | tf_op jit(solution)/shard_map/all_to_all | solution.py:20
  28.2 1.8 convolution_convert_fusion.5
  30.0 1.0 copy.24
  31.0 13.3 %all-to-all-done.1 = bf16[8,64,384]{2,0,1:T(8,128)(2,1)S(1)} async-done(((bf16[8,64,384]{2,0,1:T(8,128)(2,1)}), bf16[8,64,384]{2,0,1:T(8,128)(2,1)S(1)}, u32[]{:S(2)}, u32[]{:S(2)}) %all-to-all-start.1) | async-done | bytes 393248 | tf_op jit(solution)/shard_map/all_to_all | solution.py:20
  44.3 4.4 all-to-all-start
  48.6 0.0 reduce-scatter.3.cloned.1.call-start
  48.7 2.6 convolution_bitcast_fusion
  51.3 12.5 %all-to-all-done = bf16[8,64,384]{2,0,1:T(8,128)(2,1)} async-done(((bf16[8,64,384]{2,0,1:T(8,128)(2,1)}), bf16[8,64,384]{2,0,1:T(8,128)(2,1)}, u32[]{:S(2)}, u32[]{:S(2)}) %all-to-all-start) | async-done | bytes 393248 | tf_op jit(solution)/shard_map/all_to_all | solution.py:21
  63.9 5.2 fusion.8
  69.1 1.1 copy-done.3
  70.2 2.5 convolution_convert_fusion.1
  72.7 0.0 reduce-scatter.3.cloned.1.call-update
  72.7 0.0 reduce-scatter.5.cloned.1.call-start
  72.7 4.7 convolution_convert_fusion
  77.5 0.0 reduce-scatter.5.cloned.1.call-update
  77.5 2.4 fusion.15
  79.9 1.2 copy.29
  81.0 3.8 all-to-all-start.2
  84.9 3.9 fusion.16
  88.8 1.2 copy.32
  89.9 14.2 %all-to-all-done.2 = bf16[256,2,384]{2,1,0:T(2,128)(2,1)S(1)} async-done(((bf16[256,2,384]{2,1,0:T(2,128)(2,1)}), bf16[256,2,384]{2,1,0:T(2,128)(2,1)S(1)}, u32[]{:S(2)}, u32[]{:S(2)}) %all-to-all-start.2) | async-done | bytes 393248 | tf_op jit(solution)/shard_map/all_to_all | solution.py:38
  104.2 4.0 all-to-all-start.3
  108.2 0.0 all-gather.3.cloned.1.call-start
  108.3 0.3 copy.75
  108.6 0.1 all_to_all.63
  108.7 19.4 %all-to-all-done.3 = bf16[256,2,384]{2,1,0:T(2,128)(2,1)S(1)} async-done(((bf16[256,2,384]{2,1,0:T(2,128)(2,1)}), bf16[256,2,384]{2,1,0:T(2,128)(2,1)S(1)}, u32[]{:S(2)}, u32[]{:S(2)}) %all-to-all-start.3) | async-done | bytes 393248 | tf_op jit(solution)/shard_map/all_to_all | solution.py:37
  128.1 0.3 copy.74
  128.4 0.1 all_to_all.67
  128.6 2.0 convolution_bitcast_fusion.2
  130.6 0.8 fusion.13
  131.4 0.6 convolution_bitcast_fusion.3
  132.1 3.5 convolution_bitcast_fusion.4
  135.6 0.0 all-gather.3.cloned.1.call-update
  135.6 2.6 fusion.40
  138.1 4.7 add_convert_fusion
  142.8 1.2 copy.38
  144.0 1.8 convert_element_type.61
  145.8 24.1 %reduce-scatter.5.cloned.1.call-done = bf16[2,192,384]{2,1,0:T(8,128)(2,1)} async-done(((bf16[2,1536,384]{2,1,0:T(8,128)(2,1)}), bf16[2,192,384]{2,1,0:T(8,128)(2,1)}) %reduce-scatter.5.cloned.1.call-update) | async-done | bytes 294928 | tf_op jit(solution)/shard_map/reduce_scatter | solution.py:49
  169.9 1.8 convert_element_type.63
  171.8 704.2 %all-gather.3.cloned.1.call-done = f32[98304,64]{0,1:T(8,128)} async-done(((f32[384,64]{0,1:T(8,128)}), f32[98304,64]{0,1:T(8,128)}) %all-gather.3.cloned.1.call-update) | async-done | bytes 25165840 | tf_op jit(solution)/shard_map/all_gather | solution.py:69
  876.0 13.4 %copy.45 = f32[8,8,256,384]{3,2,1,0:T(8,128)S(1)} copy(f32[8,8,256,384]{3,1,2,0:T(8,128)} %bitcast.64) | data formatting | bytes 50331648
  889.3 3.7 bitcast_reduce_fusion
  (10 shorter events, 0.0 us)
Async XLA Ops:
  8.0 40.7 %copy-start = (bf16[2,384,1536]{2,1,0:T(8,128)(2,1)S(1)}, bf16[2,384,1536]{2,1,0:T(8,128)(2,1)}, u32[]{:S(2)}) copy-start(bf16[2,384,1536]{2,1,0:T(8,128)(2,1)} %param.7) | copy-start | bytes 7077892
  15.5 28.8 %all-to-all-start.1 = ((bf16[8,64,384]{2,0,1:T(8,128)(2,1)}), bf16[8,64,384]{2,0,1:T(8,128)(2,1)S(1)}, u32[]{:S(2)}, u32[]{:S(2)}) async-start(bf16[8,64,384]{2,0,1:T(8,128)(2,1)} %copy.27), calls=%async_computation.1 | async-start | bytes 786432 | tf_op jit(solution)/shard_map/all_to_all | solution.py:20
  44.3 19.6 %all-to-all-start = ((bf16[8,64,384]{2,0,1:T(8,128)(2,1)}), bf16[8,64,384]{2,0,1:T(8,128)(2,1)}, u32[]{:S(2)}, u32[]{:S(2)}) async-start(bf16[8,64,384]{2,0,1:T(8,128)(2,1)} %copy.24), calls=%async_computation | async-start | bytes 786432 | tf_op jit(solution)/shard_map/all_to_all | solution.py:21
  48.6 95.4 %reduce-scatter.3.cloned.1.call-start = ((), (), s32[]{:S(2)}) async-start(), calls=%async_computation.6 | async-start | bytes 2654208 | tf_op jit(solution)/shard_map/reduce_scatter | solution.py:46
  69.1 1.1 copy-start.3
  72.7 97.3 %reduce-scatter.5.cloned.1.call-start = ((), (), s32[]{:S(2)}) async-start(), calls=%async_computation.7 | async-start | bytes 2654208 | tf_op jit(solution)/shard_map/reduce_scatter | solution.py:49
  81.0 23.2 %all-to-all-start.2 = ((bf16[256,2,384]{2,1,0:T(2,128)(2,1)}), bf16[256,2,384]{2,1,0:T(2,128)(2,1)S(1)}, u32[]{:S(2)}, u32[]{:S(2)}) async-start(bf16[256,2,384]{2,1,0:T(2,128)(2,1)} %copy.29), calls=%async_computation.2 | async-start | bytes 786432 | tf_op jit(solution)/shard_map/all_to_all | solution.py:38
  104.2 23.9 %all-to-all-start.3 = ((bf16[256,2,384]{2,1,0:T(2,128)(2,1)}), bf16[256,2,384]{2,1,0:T(2,128)(2,1)S(1)}, u32[]{:S(2)}, u32[]{:S(2)}) async-start(bf16[256,2,384]{2,1,0:T(2,128)(2,1)} %copy.32), calls=%async_computation.3 | async-start | bytes 786432 | tf_op jit(solution)/shard_map/all_to_all | solution.py:37
  108.2 767.7 %all-gather.3.cloned.1.call-start = ((), (), s32[]{:S(2)}) async-start(), calls=%async_computation.8 | async-start | bytes 25264128 | tf_op jit(solution)/shard_map/all_gather | solution.py:69
  128.6 2.9 copy-start.2
  132.1 6.1 copy-start.4
  889.3 3.7 copy-start.1
Sparse Core Ops, SparseCore 0:
  72.8 49.4 reduce-scatter.2
  124.9 45.0 reduce-scatter.4
Sparse Core Ops, SparseCore 1:
  135.7 740.2 all-gather.2
